TPU v7x, 256 devices: a whole 4x4x8 slice. The times are simulated.
256 devices in a mesh: rows: 32 (over y, x, core), cols: 8 (over z).
Axes of the slice: x: 4, y: 4, z: 8, core: 2. Of those that a mesh axis runs over, the one named last changes fastest.
Arguments:
- sheet: bfloat16 [16, 4096, 1024], P('cols', 'rows'), may hold values from -600 to 600
- w_in: bfloat16 [1024, 16, 384], P(None, 'cols'), may hold values from -0.1875 to 0.1875
- w_out: bfloat16 [16, 128, 1024], P('cols'), may hold values from -0.125 to 0.125
Outputs:
- mixed: bfloat16 [16, 4096, 1024], P('cols', 'rows')
All inputs are finite; a program needn't handle non-finite values.
Results may differ from a plain program's by a relative error of at most 0.0067.
Values may be sent and summed in bfloat16 or wider, within the bound.
No kernel may reach another device: no remote copies, remote signals or barrier semaphores. Data moves between devices by JAX's collectives and lax.ppermute only.
A program may use at most 128 MiB of HBM per device.

v0:
```python
import jax
import jax.numpy as jnp
import numpy as np
from jax import lax
from jax.sharding import Mesh, PartitionSpec as P

ROWS_AXES = ("y", "x", "core")


def head_norm(values):
    return values * lax.rsqrt(jnp.mean(values * values, axis=-1, keepdims=True) + 1e-06)


def feature_map(values):
    return jax.nn.elu(values) + 1.0


def finish_proj(proj):
    parts = [
        head_norm(proj[..., 0, :]),
        head_norm(proj[..., 1, :]),
        proj[..., 2, :],
        feature_map(proj[..., 3, :]),
        feature_map(proj[..., 4, :]),
        proj[..., 5, :],
    ]
    return jnp.stack(parts, axis=-2).astype(jnp.bfloat16)


def masked_prefix(gathered, mine):
    idx = lax.broadcasted_iota(jnp.int32, gathered.shape, 0)
    before = jnp.sum(jnp.where(idx < mine, gathered, 0.0), axis=0)
    return (before, jnp.sum(gathered, axis=0))


def exclusive_rows_scan(states):
    core = lax.axis_index("core")
    pair = lax.all_gather(states, "core")
    total = pair[0] + pair[1]
    own = jnp.where(core == 1, pair[0], jnp.zeros_like(pair[0]))
    half = total.shape[0] // 2
    mine = lax.dynamic_slice_in_dim(total, core * half, half, axis=0)
    gx = lax.all_gather(mine, "x")
    xpre, xsum = masked_prefix(gx, lax.axis_index("x"))
    gy = lax.all_gather(xsum, "y")
    ypre, _ = masked_prefix(gy, lax.axis_index("y"))
    chip_prefix = lax.all_gather(ypre + xpre, "core", axis=0, tiled=True)
    return chip_prefix + own


def body(sheet, w_in, w_out):
    high = lax.Precision.HIGHEST
    width = sheet.shape[2]
    heads_here = w_in.shape[1]
    hdim = w_out.shape[1] // 2
    ncols = lax.axis_size("cols")
    core = lax.axis_index("core")
    wh = width // 2
    w_part = lax.dynamic_slice_in_dim(w_out, core * wh, wh, axis=2)
    w_part = lax.all_gather(w_part, "cols", axis=0, tiled=True)
    w_full = lax.all_gather(w_part, "core", axis=2, tiled=True)
    xloc = sheet.astype(jnp.float32)
    normed = (xloc * lax.rsqrt(jnp.mean(xloc * xloc, axis=-1, keepdims=True) + 1e-06)).astype(
        jnp.bfloat16
    )
    piece = lax.all_gather(normed, "cols", axis=0, tiled=True)
    w_flat = w_in.reshape(width, heads_here * 6 * hdim)
    proj = jnp.dot(piece.reshape(-1, width), w_flat, preferred_element_type=jnp.float32)
    all_cols, row_count = (piece.shape[0], piece.shape[1])
    parts = finish_proj(proj.reshape(all_cols, row_count, heads_here, 6, hdim))
    qrow, krow, vrow = (parts[:, :, :, 0], parts[:, :, :, 1], parts[:, :, :, 2])
    fq, fk, vcol = (parts[:, :, :, 3], parts[:, :, :, 4], parts[:, :, :, 5])
    states = jnp.einsum("crhk,crhv->chkv", fk, vcol, preferred_element_type=jnp.float32)
    prior = exclusive_rows_scan(states)
    scale = hdim ** (-0.5)
    score = jnp.einsum("crhd,erhd->rhce", qrow, krow, preferred_element_type=jnp.float32) * scale
    expo = jnp.exp(score)
    weights = (expo / jnp.sum(expo, axis=-1, keepdims=True)).astype(jnp.bfloat16)
    orow = jnp.einsum("rhce,erhd->crhd", weights, vrow, preferred_element_type=jnp.float32).astype(
        jnp.bfloat16
    )
    causal = (jnp.arange(row_count)[:, None] >= jnp.arange(row_count)[None, :]).astype(jnp.float32)
    inner = jnp.einsum("cthd,cshd->chts", fq, fk, preferred_element_type=jnp.float32) * causal
    local = jnp.einsum("chts,cshv->cthv", inner, vcol.astype(jnp.float32), precision=high)
    carried = jnp.einsum("cthk,chkv->cthv", fq.astype(jnp.float32), prior, precision=high)
    ocol = head_norm(carried + local).astype(jnp.bfloat16)
    results = jnp.concatenate([orow, ocol], axis=3)
    mine = lax.all_to_all(results, "cols", 0, 2, tiled=True)
    own_cols = mine.shape[0]
    mixed = jnp.dot(
        mine.reshape(own_cols * row_count, -1),
        w_full.reshape(-1, width),
        preferred_element_type=jnp.float32,
    )
    return mixed.reshape(own_cols, row_count, width).astype(jnp.bfloat16)


def split_mesh(mesh):
    devs = mesh.devices
    n_rows, n_cols = devs.shape
    try:
        nx = len({d.coords[0] for d in devs.flat})
    except Exception:
        nx = 4
    ny = n_rows // (nx * 2)
    return Mesh(devs.reshape(ny, nx, 2, n_cols), ROWS_AXES + ("cols",))


def solution(mesh):
    m4 = split_mesh(mesh)
    spec = P("cols", ROWS_AXES, None)
    return jax.shard_map(
        body,
        mesh=m4,
        in_specs=(spec, P(None, "cols", None), P("cols", None, None)),
        out_specs=spec,
        check_vma=False,
    )
```

profile of v0, /device:TPU:2, one launch (start us, length us, event | category | flops | bytes accessed | tf_op | source)
XLA Modules:
  0.0 267.3 jit_solution(8593396329968372122)
XLA Ops:
  6.5 1.3 fusion.10
  7.8 2.0 fusion.11
  9.9 1.7 copy.59
  11.6 1.6 copy.38
  13.3 54.4 %all-gather.10.cloned.1.call-done = bf16[16,128,1024]{2,1,0:T(8,128)(2,1)} async-done(((bf16[2,128,1024]{2,1,0:T(8,128)(2,1)}), bf16[16,128,1024]{2,1,0:T(8,128)(2,1)}) %all-gather.10.cloned.1.call-update) | async-done | bytes 4194320 | tf_op jit(solution)/shard_map/all_gather | solution.py:66
  67.7 5.8 %fusion.43 = (bf16[16,128,2,6,64]{1,4,3,2,0:T(8,128)(2,1)S(1)}, f32[16,128,2,6,64]{1,4,3,2,0:T(8,128)S(1)}) fusion(bf16[2,6,64,1024,1]{3,2,1,0,4:T(8,128)(2,1)} %bitcast.62, bf16[16,128,1024]{2,1,0:T(8,128)(2,1)} %all-gather.10.cloned.1.call-done), kind=kOutput, calls=%fused_computation.67 | convolution fusion | flops 3222798336 | bytes 15204352 | tf_op jit(solution)/shard_map/dot_general | solution.py:68
  73.5 2.6 copy-done.2
  77.1 1.5 fusion.26
  78.7 14.6 %all-gather.16.cloned.1.call-done = f32[32,2,64,64]{3,2,1,0:T(8,128)} async-done(((f32[16,2,64,64]{3,2,1,0:T(8,128)}), f32[32,2,64,64]{3,2,1,0:T(8,128)}) %all-gather.16.cloned.1.call-update) | async-done | bytes 1048592 | tf_op jit(solution)/shard_map/all_gather | solution.py:38
  93.4 1.7 fusion.42
  96.8 32.9 %all-gather.20.cloned.1.call-done = f32[32,2,64,64]{3,2,1,0:T(8,128)} async-done(((f32[8,2,64,64]{3,2,1,0:T(8,128)}), f32[32,2,64,64]{3,2,1,0:T(8,128)}) %all-gather.20.cloned.1.call-update) | async-done | bytes 1048592 | tf_op jit(solution)/shard_map/all_gather | solution.py:43
  129.7 3.1 %select_reduce_fusion = (f32[8,2,64,64]{3,2,1,0:T(8,128)}, f32[8,2,64,64]{3,2,1,0:T(8,128)}) fusion(f32[4,8,2,64,64]{4,3,2,1,0:T(8,128)} %bitcast.59, pred[4]{0:T(512)(128)(4,1)S(1)} %iota_compare_fusion.1), kind=kLoop, calls=%fused_computation.8 | loop fusion | flops 655360 | bytes 1572868 | tf_op jit(solution)/shard_map/reduce_sum | solution.py:32
  133.1 40.2 %all-gather.12.cloned.1.call-done = bf16[16,128,512]{2,1,0:T(8,128)(2,1)} async-done(((bf16[2,128,512]{2,1,0:T(8,128)(2,1)}), bf16[16,128,512]{2,1,0:T(8,128)(2,1)}) %all-gather.12.cloned.1.call-update) | async-done | bytes 2097168 | tf_op jit(solution)/shard_map/all_gather | solution.py:60
  173.3 1.9 multiply_reduce_fusion.1
  175.2 1.1 slice_bitcast_fusion.1
  176.3 1.9 fusion.21
  178.2 2.5 copy.43
  180.7 2.5 copy.44
  183.2 2.2 fusion.44
  185.5 1.3 copy.45
  187.0 1.4 copy.47
  188.4 1.6 copy.46
  190.1 1.7 fusion.45
  191.7 3.0 %copy.48 = bf16[128,2,64,16]{0,2,1,3:T(8,128)(2,1)} copy(bf16[128,2,64,16]{2,3,1,0:T(8,128)(2,1)} %fusion.45) | data formatting | bytes 1048576 | tf_op jit(solution)/shard_map/rhce,erhd->crhd/dot_general | solution.py:79
  194.7 2.6 fusion.37
  197.4 9.5 %all-gather.18.cloned.1.call-done = f32[32,2,64,64]{3,2,1,0:T(8,128)} async-done(((f32[8,2,64,64]{3,2,1,0:T(8,128)}), f32[32,2,64,64]{3,2,1,0:T(8,128)}) %all-gather.18.cloned.1.call-update) | async-done | bytes 1048592 | tf_op jit(solution)/shard_map/all_gather | solution.py:45
  206.9 2.0 select_reduce_fusion.1
  208.9 2.9 %all_gather.34 = f32[16,2,64,64]{3,2,1,0:T(8,128)S(1)} all-gather(f32[8,2,64,64]{3,2,1,0:T(8,128)S(1)} %add.72), channel_id=1, replica_groups=mesh['y'=4,'x'=4,'core'=2,'cols'=8] {'core'}, dimensions={0}, use_global_device_ids=true | all-gather | bytes 786432 | tf_op jit(solution)/shard_map/all_gather | solution.py:47
  211.8 2.6 fusion.18
  214.4 3.3 %multiply_reduce_fusion = (f32[16,128,2]{1,2,0:T(2,128)S(1)}, f32[16,128,2,64]{1,3,2,0:T(8,128)S(1)}) fusion(f32[16,2,64,128]{3,2,1,0:T(8,128)S(1)} %fusion.18, f32[16,2,128,128]{3,2,1,0:T(8,128)S(1)} %fusion.37, f32[128,128]{1,0:T(8,128)S(1)} %fusion.28, bf16[16,128,2,6,64]{1,4,3,2,0:T(8,128)(2,1)} %copy-done.5), kind=kOutput, calls=%fused_computation.28 | convolution fusion | flops 403959808 | bytes 4800512 | tf_op jit(solution)/shard_map/chts,cshv->cthv/dot_general | solution.py:84
  218.8 35.8 %all_to_all.15 = bf16[16,128,2,128]{3,2,1,0:T(2,128)(2,1)S(1)} all-to-all(bf16[16,128,2,128]{3,2,1,0:T(2,128)(2,1)S(1)} %copy.53), channel_id=1, replica_groups=mesh['y'=4,'x'=4,'core'=2,'cols'=8] {'cols'}, dimensions={0} | all-to-all | bytes 2097152 | tf_op jit(solution)/shard_map/all_to_all | solution.py:88
  256.3 4.2 %convolution_convert_fusion = bf16[2,128,1024]{2,1,0:T(8,128)(2,1)} fusion(bf16[2,128,2048]{2,1,0:T(8,128)(2,1)S(1)} %dot_general.39, bf16[2048,1024,1]{1,0,2:T(8,128)(2,1)} %bitcast.63), kind=kOutput, calls=%fused_computation.14 | convolution fusion | flops 1074003968 | bytes 5767168 | tf_op jit(solution)/shard_map/dot_general | solution.py:90
  (43 shorter events, 6.0 us)
Async XLA Ops:
  6.5 89.4 %copy-start = (bf16[2,128,1024]{2,1,0:T(8,128)(2,1)S(1)}, bf16[2,128,1024]{2,1,0:T(8,128)(2,1)}, u32[]{:S(2)}) copy-start(bf16[2,128,1024]{2,1,0:T(8,128)(2,1)} %param.5) | copy-start | bytes 1572868
  6.5 61.2 %all-gather.10.cloned.1.call-start = ((), (), s32[]{:S(2)}) async-start(), calls=%async_computation.1 | async-start | bytes 4718592 | tf_op jit(solution)/shard_map/all_gather | solution.py:66
  9.8 83.5 %all-gather.16.cloned.1.call-start = ((), (), s32[]{:S(2)}) async-start(), calls=%async_computation.4 | async-start | bytes 3145728 | tf_op jit(solution)/shard_map/all_gather | solution.py:38
  73.5 2.7 copy-start.2
  73.5 3.6 %copy-start.5 = (bf16[16,128,2,6,64]{1,4,3,2,0:T(8,128)(2,1)}, bf16[16,128,2,6,64]{1,4,3,2,0:T(8,128)(2,1)S(1)}, u32[]{:S(2)}) copy-start(bf16[16,128,2,6,64]{1,4,3,2,0:T(8,128)(2,1)S(1)} %get-tuple-element.13) | copy-start | bytes 9437188
  78.7 51.0 %all-gather.20.cloned.1.call-start = ((), (), s32[]{:S(2)}) async-start(), calls=%async_computation.6 | async-start | bytes 2621440 | tf_op jit(solution)/shard_map/all_gather | solution.py:43
  95.9 77.3 %all-gather.12.cloned.1.call-start = ((), (), s32[]{:S(2)}) async-start(), calls=%async_computation.2 | async-start | bytes 2359296 | tf_op jit(solution)/shard_map/all_gather | solution.py:60
  96.8 110.1 %all-gather.18.cloned.1.call-start = ((), (), s32[]{:S(2)}) async-start(), calls=%async_computation.5 | async-start | bytes 2621440 | tf_op jit(solution)/shard_map/all_gather | solution.py:45
  132.8 123.4 %all-gather.14.cloned.1.call-start = ((), (), s32[]{:S(2)}) async-start(), calls=%async_computation.3 | async-start | bytes 6291456 | tf_op jit(solution)/shard_map/all_gather | solution.py:61
  197.4 11.5 %copy-start.3 = (f32[8,2,64,64]{3,2,1,0:T(8,128)S(1)}, f32[8,2,64,64]{3,2,1,0:T(8,128)}, u32[]{:S(2)}) copy-start(f32[8,2,64,64]{3,2,1,0:T(8,128)} %get-tuple-element.7) | copy-start | bytes 786436
  208.8 3.0 %copy-start.1 = (f32[32,2,64,64]{3,2,1,0:T(8,128)S(1)}, f32[32,2,64,64]{3,2,1,0:T(8,128)}, u32[]{:S(2)}) copy-start(f32[32,2,64,64]{3,2,1,0:T(8,128)} %all-gather.16.cloned.1.call-done) | copy-start | bytes 3145732
  214.4 3.5 %copy-start.4 = (bf16[128,2,64,16]{0,2,1,3:T(8,128)(2,1)S(1)}, bf16[128,2,64,16]{0,2,1,3:T(8,128)(2,1)}, u32[]{:S(2)}) copy-start(bf16[128,2,64,16]{0,2,1,3:T(8,128)(2,1)} %copy.48) | copy-start | bytes 1572868
Sparse Core Ops, SparseCore 0:
  10.0 57.6 all-gather.9
  78.8 14.5 all-gather.15
  96.0 33.6 all-gather.19
  131.4 41.8 all-gather.11
  174.9 31.8 all-gather.17
  208.5 19.0 all-gather.13
where the time goes:
time: 268 us; the launch traced here: 267 us
  waiting for transfers between devices  152 us (57%)
  blocking collectives  38.7 us (14%)
  local copies, waits for them, and re-layouts  25.3 us (9%)
  matrix products  24 us (9%)
  between operations  13.8 us (5%)
  other arithmetic  13.4 us (5%)
    all_gather x1, waiting for transfers between devices, body(): piece = lax.all_gather(normed, 'cols', axis=0, tiled=True)  54.4 us
    all_gather x1, waiting for transfers between devices, body(): w_part = lax.all_gather(w_part, 'cols', axis=0, tiled=True)  40.2 us
    all_to_all x1, blocking collectives, body(): mine = lax.all_to_all(results, 'cols', 0, 2, tiled=True)  35.8 us
    all_gather x1, waiting for transfers between devices, exclusive_rows_scan(): gx = lax.all_gather(mine, 'x')  32.9 us
    all_gather x1, waiting for transfers between devices, exclusive_rows_scan(): pair = lax.all_gather(states, 'core')  14.6 us
    all_gather x1, waiting for transfers between devices, exclusive_rows_scan(): gy = lax.all_gather(xsum, 'y')  9.49 us
    squeeze x4, local copies, waits for them, and re-layouts, body(): qrow, krow, vrow = (parts[:, :, :, 0], parts[:, :, :, 1], parts[:, :, :, 2])  7.74 us
    dot_general x1, matrix products, body(): jnp.dot(piece.reshape(-1, width), w_flat, preferred_element_type=jnp.floa...  5.78 us
  transfers between devices with their start and end apart: 6, of which 5 were waited for; matrix products, arithmetic and copies ran while one was open for 16% of the time, Pallas kernels for 0%

commit v1 on v0

--- a/solution.py
+++ b/solution.py
@@ -5,6 +5,22 @@
 from jax.sharding import Mesh, PartitionSpec as P
 
 ROWS_AXES = ("y", "x", "core")
+
+
+def balance_series_all(page, mesh_dim="cols"):
+    slots = lax.axis_size(mesh_dim)
+    runs = tuple(((it, (it + 1) % slots) for it in range(slots)))
+    val, part_now = ([page], [page])
+    panels = tuple(((it, (it - 1) % slots) for it in range(slots)))
+    for _ in range(slots // 2):
+        passed = lax.ppermute(val[-1], mesh_dim, runs)
+        val.append(passed)
+    for _ in range((slots - 1) // 2):
+        front = lax.ppermute(part_now[-1], mesh_dim, panels)
+        part_now.append(front)
+    r2 = jnp.concatenate([*val[::-1], *part_now[1:]], axis=0)
+    carry_in = jnp.roll(r2, (lax.axis_index(mesh_dim) - slots // 2) * page.shape[0], axis=0)
+    return carry_in
 
 
 def head_norm(values):
@@ -57,7 +73,7 @@
     core = lax.axis_index("core")
     wh = width // 2
     w_part = lax.dynamic_slice_in_dim(w_out, core * wh, wh, axis=2)
-    w_part = lax.all_gather(w_part, "cols", axis=0, tiled=True)
+    w_part = balance_series_all(w_part)
     w_full = lax.all_gather(w_part, "core", axis=2, tiled=True)
     xloc = sheet.astype(jnp.float32)
     normed = (xloc * lax.rsqrt(jnp.mean(xloc * xloc, axis=-1, keepdims=True) + 1e-06)).astype(

time: 268 us -> 230 us (0.86)
  waiting for transfers between devices: 152 us -> 90.7 us
  local copies, waits for them, and re-layouts: 25.3 us -> 38.2 us
  starting transfers between devices: 0.39 us -> 10.4 us
    all_gather x1 -> x0, waiting for transfers between devices: 40.2 us -> none  [body(): w_part = lax.all_gather(w_part, 'cols', axis=0, tiled=True)]
    all_gather x1, waiting for transfers between devices: 32.9 us -> 3.29 us  [exclusive_rows_scan(): gx = lax.all_gather(mine, 'x')]
    ppermute x0 -> x7, waiting for transfers between devices: none -> 17.5 us  [the longest x4 17.5 us: balance_series_all(): passed = lax.ppermute(val[-1], mesh_dim, runs)]
    unnamed x13 -> x30, local copies, waits for them, and re-layouts: 5.35 us -> 16.3 us
    ppermute x0 -> x7, starting transfers between devices: none -> 10.1 us  [the longest x3 8.36 us: balance_series_all(): front = lax.ppermute(part_now[-1], mesh_dim, panels)]
    all_gather x1, waiting for transfers between devices: 9.49 us -> 0.01 us  [exclusive_rows_scan(): gy = lax.all_gather(xsum, 'y')]
    dynamic_slice x0 -> x1, local copies, waits for them, and re-layouts: none -> 3.08 us  [balance_series_all(): jnp.roll(r2, (lax.axis_index(mesh_dim) - slots // 2) * page.shape[0], axi...]
  transfers between devices with their start and end apart: 6 -> 12, of which waited for: 5 -> 6; matrix products, arithmetic and copies ran while one was open for 16% -> 25% of each run, Pallas kernels for 0% -> 0%
where the time goes in v1:
time: 230 us; the launch traced here: 229 us
  waiting for transfers between devices  90.7 us (39%)
  blocking collectives  38.8 us (17%)
  local copies, waits for them, and re-layouts  38.2 us (17%)
  matrix products  23.8 us (10%)
  other arithmetic  13.5 us (6%)
  between operations  13.5 us (6%)
  starting transfers between devices  10.4 us (5%)
    all_gather x1, waiting for transfers between devices, body(): piece = lax.all_gather(normed, 'cols', axis=0, tiled=True)  55.3 us
    all_to_all x1, blocking collectives, body(): mine = lax.all_to_all(results, 'cols', 0, 2, tiled=True)  35.8 us
    ppermute x4, waiting for transfers between devices, balance_series_all(): passed = lax.ppermute(val[-1], mesh_dim, runs)  17.5 us
    unnamed x30, local copies, waits for them, and re-layouts  16.3 us
    all_gather x1, waiting for transfers between devices, exclusive_rows_scan(): pair = lax.all_gather(states, 'core')  14.5 us
    squeeze x4, local copies, waits for them, and re-layouts, body(): qrow, krow, vrow = (parts[:, :, :, 0], parts[:, :, :, 1], parts[:, :, :, 2])  8.56 us
    ppermute x3, starting transfers between devices, balance_series_all(): front = lax.ppermute(part_now[-1], mesh_dim, panels)  8.36 us
    dot_general x1, matrix products, body(): jnp.dot(piece.reshape(-1, width), w_flat, preferred_element_type=jnp.floa...  5.38 us
  transfers between devices with their start and end apart: 12, of which 6 were waited for; matrix products, arithmetic and copies ran while one was open for 25% of the time, Pallas kernels for 0%

profile of v1, /device:TPU:2, one launch (start us, length us, event | category | flops | bytes accessed | tf_op | source)
XLA Modules:
  0.0 228.8 jit_solution(2684376724711382173)
XLA Ops:
  7.8 2.0 fusion.11
  9.8 1.7 copy.59
  12.3 55.3 %all-gather.9.cloned.1.call-done = bf16[16,128,1024]{2,1,0:T(8,128)(2,1)} async-done(((bf16[2,128,1024]{2,1,0:T(8,128)(2,1)}), bf16[16,128,1024]{2,1,0:T(8,128)(2,1)}) %all-gather.9.cloned.1.call-update) | async-done | bytes 4194320 | tf_op jit(solution)/shard_map/all_gather | solution.py:82
  67.6 5.4 %fusion.43 = (bf16[16,128,2,6,64]{1,4,3,2,0:T(8,128)(2,1)S(1)}, f32[16,128,2,6,64]{1,4,3,2,0:T(8,128)S(1)}) fusion(bf16[2,6,64,1024,1]{3,2,1,0,4:T(8,128)(2,1)S(1)} %bitcast.62, bf16[16,128,1024]{2,1,0:T(8,128)(2,1)} %all-gather.9.cloned.1.call-done), kind=kOutput, calls=%fused_computation.84 | convolution fusion | flops 3222798336 | bytes 15204352 | tf_op jit(solution)/shard_map/dot_general | solution.py:84
  73.1 2.6 %copy-done.1 = f32[16,128,2,6,64]{1,4,3,2,0:T(8,128)} copy-done((f32[16,128,2,6,64]{1,4,3,2,0:T(8,128)}, f32[16,128,2,6,64]{1,4,3,2,0:T(8,128)S(1)}, u32[]{:S(2)}) %copy-start.1) | copy-done | bytes 6291480
  78.5 14.5 %all-gather.13.cloned.1.call-done = f32[32,2,64,64]{3,2,1,0:T(8,128)} async-done(((f32[16,2,64,64]{3,2,1,0:T(8,128)}), f32[32,2,64,64]{3,2,1,0:T(8,128)}) %all-gather.13.cloned.1.call-update) | async-done | bytes 1048592 | tf_op jit(solution)/shard_map/all_gather | solution.py:54
  92.9 1.7 fusion.42
  95.6 1.6 collective-permute-start.1
  97.2 1.8 collective-permute-start.4
  99.0 6.7 %collective-permute-done.1 = bf16[2,128,512]{2,1,0:T(8,128)(2,1)S(1)} collective-permute-done((bf16[2,128,512]{2,1,0:T(8,128)(2,1)S(1)}, bf16[2,128,512]{2,1,0:T(8,128)(2,1)S(1)}, u32[]{:S(2)}, u32[]{:S(2)}) %collective-permute-start.1) | collective-permute-done | bytes 262176 | tf_op jit(solution)/shard_map/ppermute | solution.py:16
  105.7 3.2 %collective-permute-start.5 = (bf16[2,128,512]{2,1,0:T(8,128)(2,1)S(1)}, bf16[2,128,512]{2,1,0:T(8,128)(2,1)S(1)}, u32[]{:S(2)}, u32[]{:S(2)}) collective-permute-start(bf16[2,128,512]{2,1,0:T(8,128)(2,1)S(1)} %collective-permute-done.4), channel_id=1, source_target_pairs={{0,7},{1,0},{2,1},{3,2},{4,3},{5,4},{6,5},{7,6},{8,15},{9,8},{10,9... | collective-permute-start | bytes 786440 | tf_op jit(solution)/shard_map/ppermute | solution.py:19
  108.9 5.9 %collective-permute-done.2 = bf16[2,128,512]{2,1,0:T(8,128)(2,1)S(1)} collective-permute-done((bf16[2,128,512]{2,1,0:T(8,128)(2,1)S(1)}, bf16[2,128,512]{2,1,0:T(8,128)(2,1)S(1)}, u32[]{:S(2)}, u32[]{:S(2)}) %collective-permute-start.2) | collective-permute-done | bytes 262176 | tf_op jit(solution)/shard_map/ppermute | solution.py:16
  114.9 3.3 %collective-permute-start.6 = (bf16[2,128,512]{2,1,0:T(8,128)(2,1)S(1)}, bf16[2,128,512]{2,1,0:T(8,128)(2,1)S(1)}, u32[]{:S(2)}, u32[]{:S(2)}) collective-permute-start(bf16[2,128,512]{2,1,0:T(8,128)(2,1)S(1)} %collective-permute-done.5), channel_id=1, source_target_pairs={{0,7},{1,0},{2,1},{3,2},{4,3},{5,4},{6,5},{7,6},{8,15},{9,8},{10,9... | collective-permute-start | bytes 786440 | tf_op jit(solution)/shard_map/ppermute | solution.py:19
  118.2 4.9 %collective-permute-done.3 = bf16[2,128,512]{2,1,0:T(8,128)(2,1)S(1)} collective-permute-done((bf16[2,128,512]{2,1,0:T(8,128)(2,1)S(1)}, bf16[2,128,512]{2,1,0:T(8,128)(2,1)S(1)}, u32[]{:S(2)}, u32[]{:S(2)}) %collective-permute-start.3) | collective-permute-done | bytes 262176 | tf_op jit(solution)/shard_map/ppermute | solution.py:16
  126.0 3.3 %all-gather.17.cloned.1.call-done = f32[32,2,64,64]{3,2,1,0:T(8,128)} async-done(((f32[8,2,64,64]{3,2,1,0:T(8,128)}), f32[32,2,64,64]{3,2,1,0:T(8,128)}) %all-gather.17.cloned.1.call-update) | async-done | bytes 1048592 | tf_op jit(solution)/shard_map/all_gather | solution.py:59
  129.3 3.1 %select_reduce_fusion = (f32[8,2,64,64]{3,2,1,0:T(8,128)}, f32[8,2,64,64]{3,2,1,0:T(8,128)}) fusion(f32[4,8,2,64,64]{4,3,2,1,0:T(8,128)} %bitcast.58, pred[4]{0:T(512)(128)(4,1)S(1)} %iota_compare_fusion.1), kind=kLoop, calls=%fused_computation.8 | loop fusion | flops 655360 | bytes 1572868 | tf_op jit(solution)/shard_map/reduce_sum | solution.py:48
  141.5 3.1 %constant_dynamic-slice_fusion = bf16[16,128,512]{2,1,0:T(8,128)(2,1)} fusion(bf16[32,128,512]{2,1,0:T(8,128)(2,1)} %constant_dynamic-update-slice_fusion, s32[]{:T(128)S(6)} %select_n.69), kind=kLoop, calls=%fused_computation.75 | loop fusion | bytes 4194308 | tf_op jit(solution)/shard_map/jit(_roll_dynamic)/dynamic_slice | solution.py:22
  144.6 2.0 multiply_reduce_fusion.1
  146.6 1.9 slice_bitcast_fusion.1
  148.6 1.9 fusion.21
  150.5 1.6 copy.43
  152.1 2.5 %copy.44 = bf16[16,128,2,64]{3,0,2,1:T(8,128)(2,1)} copy(bf16[16,128,2,64]{1,3,2,0:T(8,128)(2,1)S(1)} %get-tuple-element.9) | data formatting | bytes 1048576 | tf_op jit(solution)/shard_map/squeeze | solution.py:87
  154.7 1.9 fusion.44
  159.5 2.5 %copy.46 = bf16[16,128,2,64]{3,0,2,1:T(8,128)(2,1)S(1)} copy(bf16[16,128,2,64]{1,3,2,0:T(8,128)(2,1)} %slice_bitcast_fusion.1) | data formatting | bytes 1048576 | tf_op jit(solution)/shard_map/squeeze | solution.py:87
  162.7 1.8 copy.48
  164.5 4.1 %fusion.37 = f32[16,2,128,128]{3,2,1,0:T(8,128)} fusion(f32[16,128,2,6,64]{1,4,3,2,0:T(8,128)} %copy-done.1), kind=kOutput, calls=%fused_computation.82 | convolution fusion | flops 69730304 | bytes 4194304 | tf_op jit(solution)/shard_map/cthd,cshd->chts/dot_general | solution.py:99
  168.6 2.0 select_reduce_fusion.1
  170.7 2.9 %all_gather.31 = f32[16,2,64,64]{3,2,1,0:T(8,128)S(1)} all-gather(f32[8,2,64,64]{3,2,1,0:T(8,128)S(1)} %add.83), channel_id=1, replica_groups=mesh['y'=4,'x'=4,'core'=2,'cols'=8] {'core'}, dimensions={0}, use_global_device_ids=true | all-gather | bytes 786432 | tf_op jit(solution)/shard_map/all_gather | solution.py:63
  173.6 2.6 %fusion.18 = f32[16,2,64,128]{3,2,1,0:T(8,128)S(1)} fusion(f32[16,2,64,64]{3,2,1,0:T(8,128)S(1)} %all_gather.31, pred[]{:T(512)S(6)} %eq.6, f32[32,2,64,64]{3,2,1,0:T(8,128)S(1)} %copy-done, f32[16,128,2,6,64]{1,4,3,2,0:T(8,128)} %copy-done.1), kind=kOutput, calls=%fused_computation.26 | convolution fusion | flops 202899456 | bytes 4194305 | tf_op jit(solution)/shard_map/cthk,chkv->cthv/dot_general | solution.py:101
  176.2 3.3 %multiply_reduce_fusion = (f32[16,128,2]{1,2,0:T(2,128)S(1)}, f32[16,128,2,64]{1,3,2,0:T(8,128)S(1)}) fusion(f32[16,2,64,128]{3,2,1,0:T(8,128)S(1)} %fusion.18, f32[16,2,128,128]{3,2,1,0:T(8,128)S(1)} %copy-done.2, f32[128,128]{1,0:T(8,128)S(1)} %fusion.28, bf16[16,128,2,6,64]{1,4,3,2,0:T(8,128)(2,1)} %copy-done.6), kind=kOutput, calls=%fused_computation.28 | convolution fusion | flops 403959808 | bytes 4800512 | tf_op jit(solution)/shard_map/chts,cshv->cthv/dot_general | solution.py:100
  180.6 35.8 %all_to_all.15 = bf16[16,128,2,128]{3,2,1,0:T(2,128)(2,1)S(1)} all-to-all(bf16[16,128,2,128]{3,2,1,0:T(2,128)(2,1)S(1)} %copy.53), channel_id=1, replica_groups=mesh['y'=4,'x'=4,'core'=2,'cols'=8] {'cols'}, dimensions={0} | all-to-all | bytes 2097152 | tf_op jit(solution)/shard_map/all_to_all | solution.py:104
  218.1 4.2 %convolution_convert_fusion = bf16[2,128,1024]{2,1,0:T(8,128)(2,1)} fusion(bf16[2,128,2048]{2,1,0:T(8,128)(2,1)S(1)} %dot_general.39, bf16[2048,1024,1]{1,0,2:T(8,128)(2,1)} %bitcast.63), kind=kOutput, calls=%fused_computation.14 | convolution fusion | flops 1074003968 | bytes 5767168 | tf_op jit(solution)/shard_map/dot_general | solution.py:106
  (73 shorter events, 24.0 us)
Async XLA Ops:
  6.5 61.1 %all-gather.9.cloned.1.call-start = ((), (), s32[]{:S(2)}) async-start(), calls=%async_computation.1 | async-start | bytes 4718592 | tf_op jit(solution)/shard_map/all_gather | solution.py:82
  9.8 83.1 %all-gather.13.cloned.1.call-start = ((), (), s32[]{:S(2)}) async-start(), calls=%async_computation.3 | async-start | bytes 3145728 | tf_op jit(solution)/shard_map/all_gather | solution.py:54
  67.6 10.7 %copy-start.5 = (bf16[2,128,1024]{2,1,0:T(8,128)(2,1)S(1)}, bf16[2,128,1024]{2,1,0:T(8,128)(2,1)}, u32[]{:S(2)}) copy-start(bf16[2,128,1024]{2,1,0:T(8,128)(2,1)} %param.5) | copy-start | bytes 1572868
  73.0 2.7 %copy-start.1 = (f32[16,128,2,6,64]{1,4,3,2,0:T(8,128)}, f32[16,128,2,6,64]{1,4,3,2,0:T(8,128)S(1)}, u32[]{:S(2)}) copy-start(f32[16,128,2,6,64]{1,4,3,2,0:T(8,128)S(1)} %get-tuple-element.14) | copy-start | bytes 18874372
  73.0 3.7 %copy-start.6 = (bf16[16,128,2,6,64]{1,4,3,2,0:T(8,128)(2,1)}, bf16[16,128,2,6,64]{1,4,3,2,0:T(8,128)(2,1)S(1)}, u32[]{:S(2)}) copy-start(bf16[16,128,2,6,64]{1,4,3,2,0:T(8,128)(2,1)S(1)} %get-tuple-element.13) | copy-start | bytes 9437188
  78.3 51.0 %all-gather.17.cloned.1.call-start = ((), (), s32[]{:S(2)}) async-start(), calls=%async_computation.5 | async-start | bytes 2621440 | tf_op jit(solution)/shard_map/all_gather | solution.py:59
  78.4 17.2 %collective-permute-start = (bf16[2,128,512]{2,1,0:T(8,128)(2,1)S(1)}, bf16[2,128,512]{2,1,0:T(8,128)(2,1)S(1)}, u32[]{:S(2)}, u32[]{:S(2)}) collective-permute-start(bf16[2,128,512]{2,1,0:T(8,128)(2,1)S(1)} %constant_dynamic-slice_fusion.1), channel_id=1, source_target_pairs={{0,1},{1,2},{2,3},{3,4},{4,5},{5,6},{6,7},{7,0},{8,9},{9,10},{10,1... | collective-permute-start | bytes 786440 | tf_op jit(solution)/shard_map/ppermute | solution.py:16
  95.5 73.1 %all-gather.15.cloned.1.call-start = ((), (), s32[]{:S(2)}) async-start(), calls=%async_computation.4 | async-start | bytes 2621440 | tf_op jit(solution)/shard_map/all_gather | solution.py:61
  95.6 10.2 %collective-permute-start.1 = (bf16[2,128,512]{2,1,0:T(8,128)(2,1)S(1)}, bf16[2,128,512]{2,1,0:T(8,128)(2,1)S(1)}, u32[]{:S(2)}, u32[]{:S(2)}) collective-permute-start(bf16[2,128,512]{2,1,0:T(8,128)(2,1)S(1)} %collective-permute-done), channel_id=1, source_target_pairs={{0,1},{1,2},{2,3},{3,4},{4,5},{5,6},{6,7},{7,0},{8,9},{9,10},{10,1... | collective-permute-start | bytes 786440 | tf_op jit(solution)/shard_map/ppermute | solution.py:16
  97.2 8.5 %collective-permute-start.4 = (bf16[2,128,512]{2,1,0:T(8,128)(2,1)S(1)}, bf16[2,128,512]{2,1,0:T(8,128)(2,1)S(1)}, u32[]{:S(2)}, u32[]{:S(2)}) collective-permute-start(bf16[2,128,512]{2,1,0:T(8,128)(2,1)S(1)} %constant_dynamic-slice_fusion.1), channel_id=1, source_target_pairs={{0,7},{1,0},{2,1},{3,2},{4,3},{5,4},{6,5},{7,6},{8,15},{9,8},{10,9... | collective-permute-start | bytes 786440 | tf_op jit(solution)/shard_map/ppermute | solution.py:19
  105.7 9.1 %collective-permute-start.2 = (bf16[2,128,512]{2,1,0:T(8,128)(2,1)S(1)}, bf16[2,128,512]{2,1,0:T(8,128)(2,1)S(1)}, u32[]{:S(2)}, u32[]{:S(2)}) collective-permute-start(bf16[2,128,512]{2,1,0:T(8,128)(2,1)S(1)} %collective-permute-done.1), channel_id=1, source_target_pairs={{0,1},{1,2},{2,3},{3,4},{4,5},{5,6},{6,7},{7,0},{8,9},{9,10},{10,1... | collective-permute-start | bytes 786440 | tf_op jit(solution)/shard_map/ppermute | solution.py:16
  105.7 9.2 %collective-permute-start.5 = (bf16[2,128,512]{2,1,0:T(8,128)(2,1)S(1)}, bf16[2,128,512]{2,1,0:T(8,128)(2,1)S(1)}, u32[]{:S(2)}, u32[]{:S(2)}) collective-permute-start(bf16[2,128,512]{2,1,0:T(8,128)(2,1)S(1)} %collective-permute-done.4), channel_id=1, source_target_pairs={{0,7},{1,0},{2,1},{3,2},{4,3},{5,4},{6,5},{7,6},{8,15},{9,8},{10,9... | collective-permute-start | bytes 786440 | tf_op jit(solution)/shard_map/ppermute | solution.py:19
  114.8 8.3 %collective-permute-start.3 = (bf16[2,128,512]{2,1,0:T(8,128)(2,1)S(1)}, bf16[2,128,512]{2,1,0:T(8,128)(2,1)S(1)}, u32[]{:S(2)}, u32[]{:S(2)}) collective-permute-start(bf16[2,128,512]{2,1,0:T(8,128)(2,1)S(1)} %collective-permute-done.2), channel_id=1, source_target_pairs={{0,1},{1,2},{2,3},{3,4},{4,5},{5,6},{6,7},{7,0},{8,9},{9,10},{10,1... | collective-permute-start | bytes 786440 | tf_op jit(solution)/shard_map/ppermute | solution.py:16
  114.9 19.9 %collective-permute-start.6 = (bf16[2,128,512]{2,1,0:T(8,128)(2,1)S(1)}, bf16[2,128,512]{2,1,0:T(8,128)(2,1)S(1)}, u32[]{:S(2)}, u32[]{:S(2)}) collective-permute-start(bf16[2,128,512]{2,1,0:T(8,128)(2,1)S(1)} %collective-permute-done.5), channel_id=1, source_target_pairs={{0,7},{1,0},{2,1},{3,2},{4,3},{5,4},{6,5},{7,6},{8,15},{9,8},{10,9... | collective-permute-start | bytes 786440 | tf_op jit(solution)/shard_map/ppermute | solution.py:19
  132.4 85.6 %all-gather.11.cloned.1.call-start = ((), (), s32[]{:S(2)}) async-start(), calls=%async_computation.2 | async-start | bytes 6291456 | tf_op jit(solution)/shard_map/all_gather | solution.py:77
  164.5 6.1 %copy-start.3 = (f32[8,2,64,64]{3,2,1,0:T(8,128)S(1)}, f32[8,2,64,64]{3,2,1,0:T(8,128)}, u32[]{:S(2)}) copy-start(f32[8,2,64,64]{3,2,1,0:T(8,128)} %get-tuple-element.7) | copy-start | bytes 786436
  164.5 9.1 %copy-start = (f32[32,2,64,64]{3,2,1,0:T(8,128)S(1)}, f32[32,2,64,64]{3,2,1,0:T(8,128)}, u32[]{:S(2)}) copy-start(f32[32,2,64,64]{3,2,1,0:T(8,128)} %all-gather.13.cloned.1.call-done) | copy-start | bytes 3145732
  170.6 5.6 %copy-start.2 = (f32[16,2,128,128]{3,2,1,0:T(8,128)S(1)}, f32[16,2,128,128]{3,2,1,0:T(8,128)}, u32[]{:S(2)}) copy-start(f32[16,2,128,128]{3,2,1,0:T(8,128)} %fusion.37) | copy-start | bytes 6291460
  176.2 3.5 %copy-start.4 = (bf16[128,2,64,16]{0,2,1,3:T(8,128)(2,1)S(1)}, bf16[128,2,64,16]{0,2,1,3:T(8,128)(2,1)}, u32[]{:S(2)}) copy-start(bf16[128,2,64,16]{0,2,1,3:T(8,128)(2,1)} %copy.48) | copy-start | bytes 1572868
Sparse Core Ops, SparseCore 0:
  9.9 57.6 all-gather.8
  78.4 14.5 all-gather.12
  95.6 33.6 all-gather.16
  132.6 34.3 all-gather.14
  168.6 19.0 all-gather.10
